TPU v7x, 32 devices: a whole 2x2x4 slice. The times are simulated.
32 devices in a mesh: shot: 8 (over z, y), off: 4 (over x, core).
Axes of the slice: x: 2, y: 2, z: 4, core: 2. Of those that a mesh axis runs over, the one named last changes fastest.
Arguments:
- traces: float32 [8192, 2048], P(('shot', 'off')), may hold values from -6 to 6
- cmp_bin: int32 [8192], P(('shot', 'off')), may hold values from 0 to 255, as said below
- offset_class: int32 [8192], P(('shot', 'off')), may hold values from 0 to 79, as said below
- bin_rank: int32 [256], replicated, may hold values from 0 to 255, as said below
- filter_off: float32 [7], replicated, may hold values from -2.5 to 2.5
- filter_time: float32 [65], replicated, may hold values from -2 to 2
Outputs:
- planes: float32 [80, 2048, 256], P('off', 'shot')
Inputs may be any that keep to these rules, and one draw needn't show every extreme that they name: `cmp_bin`: in each aligned block of 256 rows (the rows of one device) at most 128 rows name bins with the same owner bin_rank // 32; one owner, the same for all blocks, gets exactly 128 rows of every block, and every other owner gets a whole number of rows next to 128 / (7) (its floor or ceiling). `offset_class`: row r has a class from g * 20 to g * 20 + 19, with g = (r // 256) % 4. `bin_rank`: A permutation.
All inputs are finite; a program needn't handle non-finite values.
Results may differ from a plain program's by a relative error of at most 0.00007.
Values sent between devices are 32-bit elements; how exact they have to be, the bound alone decides.
No kernel may reach another device: no remote copies, remote signals or barrier semaphores. Data moves between devices by JAX's collectives and lax.ppermute only.
A program may use at most 128 MiB of HBM per device.

v0:
```python
import jax
import jax.numpy as jnp
from jax import lax
from jax.sharding import PartitionSpec as P

OFFC = 80
BOWN = 32


def extended_2(cells, sides, width):
    for axis, dim in sides:
        count = lax.axis_size(axis)
        ends = count - 1
        head = lax.slice_in_dim(cells, 0, width, axis=dim)
        tail = lax.slice_in_dim(cells, cells.shape[dim] - width, cells.shape[dim], axis=dim)
        cells = jnp.concatenate(
            [
                lax.ppermute(tail, axis, [(i, (i + 1) % count) for i in range(ends)]),
                cells,
                lax.ppermute(head, axis, [((i + 1) % count, i) for i in range(ends)]),
            ],
            axis=dim,
        )
    return cells


def tap_table(filter_time, width_in, width_out):
    inner = jnp.arange(width_in, dtype=jnp.int32)[:, None]
    outer = jnp.arange(width_out, dtype=jnp.int32)[None, :]
    distance = inner - outer
    taps = jnp.arange(filter_time.shape[0], dtype=jnp.int32)
    matches = distance[:, :, None] == taps[None, None, :]
    return jnp.sum(jnp.where(matches, filter_time[None, None, :], 0.0), axis=2)


def block_filter(data, filter_time):
    reach = filter_time.shape[0] // 2
    block_width = 128
    leading = data.shape[:-1]
    samples = data.shape[-1]
    blocks = data.reshape(leading + (samples // block_width, block_width))
    zeroes = jnp.zeros(leading + (1, reach), jnp.float32)
    before = jnp.concatenate([zeroes, blocks[..., :-1, block_width - reach :]], axis=-2)
    after = jnp.concatenate([blocks[..., 1:, :reach], zeroes], axis=-2)
    extended = jnp.concatenate([before, blocks, after], axis=-1)
    table = tap_table(filter_time, block_width + 2 * reach, block_width)
    result = jnp.einsum("...ki,io->...ko", extended, table, precision=lax.Precision.HIGHEST)
    return result.reshape(leading + (samples,))


def offset_mix(scaled, filter_off):
    reach = filter_off.shape[0] // 2
    padded = extended_2(scaled, (("off", 0),), reach)
    count = scaled.shape[0]
    mixed = filter_off[0] * padded[0:count]
    for offset_tap in range(1, filter_off.shape[0]):
        mixed = mixed + filter_off[offset_tap] * padded[offset_tap : offset_tap + count]
    return mixed


def stack_cells(received, labels, segments):
    stacked = jax.ops.segment_sum(received, labels, num_segments=segments + 1)[:segments]
    fold_count = jax.ops.segment_sum(
        jnp.ones(labels.shape, jnp.float32), labels, num_segments=segments + 1
    )[:segments]
    return stacked / jnp.maximum(fold_count, 1.0)[:, None]


def body(traces, cmp_bin, offset_class, bin_rank, filter_off, filter_time):
    shots = lax.axis_size("shot")
    off_dev = OFFC // lax.axis_size("off")
    first_class = lax.axis_index("off") * off_dev
    bin_count = bin_rank.shape[0]
    tr_dev = traces.shape[0]
    samples = traces.shape[1]
    matches = cmp_bin[:, None] == jnp.arange(bin_count, dtype=jnp.int32)[None, :]
    rank_of = jnp.sum(jnp.where(matches, bin_rank[None, :], 0), axis=1)
    local_class = offset_class - first_class
    capacity = max(2, 4 * tr_dev // shots)
    owning = rank_of // BOWN
    member = (owning[:, None] == jnp.arange(shots, dtype=jnp.int32)[None, :]).astype(jnp.int32)
    position = jnp.sum(jnp.cumsum(member, axis=0) * member, axis=1) - 1
    target = owning * capacity + position
    sentinel = off_dev * BOWN
    cell_index = local_class * BOWN + rank_of % BOWN
    outgoing = jnp.zeros((shots * capacity, samples), jnp.float32).at[target].set(traces)
    labels = jnp.full((shots * capacity,), sentinel, jnp.int32).at[target].set(cell_index)
    received, arrived = (
        lax.all_to_all(outgoing, "shot", split_axis=0, concat_axis=0, tiled=True),
        lax.all_to_all(labels, "shot", split_axis=0, concat_axis=0, tiled=True),
    )
    scaled = stack_cells(received, arrived, sentinel).reshape(off_dev, BOWN, samples)
    mixed = offset_mix(scaled, filter_off)
    filtered = block_filter(mixed, filter_time)
    relayed = lax.all_to_all(filtered, "shot", split_axis=2, concat_axis=1, tiled=True)
    return jnp.transpose(relayed, (0, 2, 1))


def solution(mesh):
    return jax.shard_map(
        body,
        mesh=mesh,
        in_specs=(P(("shot", "off"), None), P(("shot", "off")), P(("shot", "off")), P(), P(), P()),
        out_specs=P("off", "shot", None),
        check_vma=False,
    )
```

profile of v0, /device:TPU:1, one launch (start us, length us, event | category | flops | bytes accessed | tf_op | source)
XLA Modules:
  0.0 474.5 jit_solution(17869726358721929491)
XLA Ops:
  0.0 0.9 select_reduce_fusion.1
  0.9 0.6 reduce-window.6
  1.5 0.2 slice_reduce_fusion
  1.7 0.7 fusion.34
  2.4 0.1 fusion.28
  2.6 2.0 scatter_custom_fusion
  4.5 6.4 %all-to-all-start = ((s32[8,128,1]{1,2,0:T(1,128)}), s32[8,128,1]{1,2,0:T(1,128)S(1)}, u32[]{:S(2)}, u32[]{:S(2)}) async-start(s32[8,128,1]{1,2,0:T(1,128)} %bitcast.8), calls=%async_computation | async-start | bytes 8192 | tf_op jit(solution)/shard_map/all_to_all | solution.py:90
  10.9 6.6 %scatter_custom_fusion.1 = f32[1024,2048]{1,0:T(8,128)} fusion(s32[256]{0:T(256)S(1)} %bitcast.67, f32[256,2048]{1,0:T(8,128)} %param.6, f32[]{:T(128)} %constant.24.clone.1), kind=kCustom, calls=%fused_computation.44 | custom fusion | bytes 8389120 | tf_op jit(solution)/shard_map/scatter | solution.py:86
  17.5 0.0 all-to-all-done
  17.5 5.4 %all-to-all-start.1 = ((f32[8,128,2048]{2,1,0:T(8,128)}), f32[8,128,2048]{2,1,0:T(8,128)}, u32[]{:S(2)}, u32[]{:S(2)}) async-start(f32[8,128,2048]{2,1,0:T(8,128)} %bitcast.56), calls=%async_computation.1 | async-start | bytes 16777216 | tf_op jit(solution)/shard_map/all_to_all | solution.py:89
  22.9 8.1 %scatter_custom_fusion.3 = f32[641]{0:T(1024)S(1)} fusion(s32[1024]{0:T(1024)S(1)} %bitcast.64, f32[1024]{0:T(1024)S(1)} %broadcast.160, f32[]{:T(128)} %constant.24.clone.1), kind=kCustom, calls=%fused_computation.64 | custom fusion | flops 1024 | bytes 2568 | tf_op jit(solution)/shard_map/scatter-add | solution.py:63
  31.0 173.6 %all-to-all-done.1 = f32[8,128,2048]{2,1,0:T(8,128)} async-done(((f32[8,128,2048]{2,1,0:T(8,128)}), f32[8,128,2048]{2,1,0:T(8,128)}, u32[]{:S(2)}, u32[]{:S(2)}) %all-to-all-start.1) | async-done | bytes 8388640 | tf_op jit(solution)/shard_map/all_to_all | solution.py:89
  204.7 17.4 %scatter_custom_fusion.2 = f32[641,2048]{1,0:T(8,128)} fusion(s32[1024]{0:T(1024)S(1)} %bitcast.65, f32[1024,2048]{1,0:T(8,128)} %bitcast.11, f32[]{:T(128)} %constant.24.clone.1), kind=kCustom, calls=%fused_computation.46 | custom fusion | flops 2097152 | bytes 5251584 | tf_op jit(solution)/shard_map/scatter-add | solution.py:62
  222.0 0.0 copy-start
  222.1 0.0 copy-start.1
  222.1 3.3 slice_divide_fusion
  225.3 0.1 fusion.40
  225.5 5.4 %collective-permute-start = (f32[3,32,2048]{2,1,0:T(8,128)S(1)}, f32[3,32,2048]{2,1,0:T(8,128)S(1)}, u32[]{:S(2)}, u32[]{:S(2)}) collective-permute-start(f32[3,32,2048]{2,1,0:T(8,128)S(1)} %bitcast.61), channel_id=1, source_target_pairs={{0,1},{1,2},{2,3},{4,5},{5,6},{6,7},{8,9},{9,10},{10,11},{12,13},{... | collective-permute-start | bytes 2359304 | tf_op jit(solution)/shard_map/ppermute | solution.py:18
  230.9 2.1 collective-permute-start.1
  233.0 0.0 copy-done
  233.0 0.7 fusion.41
  233.7 0.0 copy-done.1
  233.7 0.8 select_reduce_fusion
  234.5 5.3 %collective-permute-done = f32[3,32,2048]{2,1,0:T(8,128)S(1)} collective-permute-done((f32[3,32,2048]{2,1,0:T(8,128)S(1)}, f32[3,32,2048]{2,1,0:T(8,128)S(1)}, u32[]{:S(2)}, u32[]{:S(2)}) %collective-permute-start) | collective-permute-done | bytes 786464 | tf_op jit(solution)/shard_map/ppermute | solution.py:18
  239.8 4.4 collective-permute-done.1
  244.2 8.8 %fusion.7 = f32[20,32,2048]{2,1,0:T(8,128)S(1)} fusion(f32[20,32,2048]{2,1,0:T(8,128)S(1)} %bitcast.57, f32[3,32,2048]{2,1,0:T(8,128)S(1)} %collective-permute-done.1, f32[3,32,2048]{2,1,0:T(8,128)S(1)} %collective-permute-done, f32[]{:T(128)} %bitcast.20, f32[]{:T(128)} %bitcast.19, f32[]{:T(128)} %bitcast.17, f32[]{:T(128)} %bitcast.16, f32[]{:T(128)} %bitcast.15, ...), kind=kLoop, calls=%fused_computation.25 | loop fusion | flops 24903680 | bytes 12058652 | tf_op jit(solution)/shard_map/add | solution.py:57
  253.0 1.2 copy.25
  254.2 4.2 fusion.39
  258.4 13.8 %fusion = f32[20,32,16,128]{3,2,1,0:T(8,128)} fusion(f32[20,32,15,32]{3,2,1,0:T(8,128)} %get-tuple-element.6, f32[20,32,15,32]{3,2,1,0:T(8,128)S(1)} %get-tuple-element.5, f32[20,32,16,128]{3,2,1,0:T(8,128)S(1)} %bitcast.55, f32[192,128]{1,0:T(8,128)S(1)} %select_reduce_fusion), kind=kOutput, calls=%fused_computation.5 | convolution fusion | flops 3031695360 | bytes 13041664 | tf_op jit(solution)/shard_map/...ki,io->...ko/dot_general | solution.py:47
  272.3 13.1 %copy.22 = f32[20,32,16,128]{1,0,3,2:T(8,128)} copy(f32[20,32,16,128]{3,2,1,0:T(8,128)} %fusion) | data formatting | bytes 10485760 | tf_op jit(solution)/shard_map/reshape | solution.py:48
  285.4 16.2 %reshape.172 = f32[8,1,163840]{2,1,0:T(1,128)} reshape(f32[2048,20,32]{2,1,0:T(8,128)} %bitcast.52) | data formatting | bytes 10485760
  301.6 111.8 %all_to_all.39 = f32[8,1,163840]{2,1,0:T(1,128)} all-to-all(f32[8,1,163840]{2,1,0:T(1,128)} %reshape.172), channel_id=1, replica_groups=mesh['shot'=8,'off'=4] {'shot'}, dimensions={0} | all-to-all | bytes 10485760 | tf_op jit(solution)/shard_map/all_to_all | solution.py:95
  413.3 0.5 broadcast.208
  413.9 16.8 %reduce.2 = f32[8,163840]{1,0:T(8,128)} reduce(f32[8,1,163840]{2,1,0:T(1,128)} %all_to_all.39, f32[]{:T(128)} %broadcast.208), dimensions={1}, to_apply=%all_to_all.32.reduce_sub_computation | reduce | bytes 10485764 | tf_op jit(solution)/shard_map/all_to_all | solution.py:95
  430.7 21.3 %reshape.173 = f32[2048,20,32]{2,1,0:T(8,128)} reshape(f32[8,163840]{1,0:T(8,128)} %reduce.2) | data formatting | bytes 10485760
  452.0 16.4 %copy.19 = f32[20,8,32,256]{3,2,1,0:T(8,128)} copy(f32[20,8,32,256]{2,0,3,1:T(8,128)} %bitcast.53) | data formatting | bytes 10485760 | tf_op jit(solution)/shard_map/all_to_all | solution.py:95
  468.4 5.9 %copy.20 = f32[20,256,256]{2,1,0:T(8,128)} copy(f32[20,256,256]{1,2,0:T(8,128)} %bitcast.59) | data formatting | bytes 10485760 | tf_op jit(solution)/shard_map/transpose | solution.py:96
  (9 shorter events, 0.1 us)
Async XLA Ops:
  4.5 13.0 %all-to-all-start = ((s32[8,128,1]{1,2,0:T(1,128)}), s32[8,128,1]{1,2,0:T(1,128)S(1)}, u32[]{:S(2)}, u32[]{:S(2)}) async-start(s32[8,128,1]{1,2,0:T(1,128)} %bitcast.8), calls=%async_computation | async-start | bytes 8192 | tf_op jit(solution)/shard_map/all_to_all | solution.py:90
  17.5 187.2 %all-to-all-start.1 = ((f32[8,128,2048]{2,1,0:T(8,128)}), f32[8,128,2048]{2,1,0:T(8,128)}, u32[]{:S(2)}, u32[]{:S(2)}) async-start(f32[8,128,2048]{2,1,0:T(8,128)} %bitcast.56), calls=%async_computation.1 | async-start | bytes 16777216 | tf_op jit(solution)/shard_map/all_to_all | solution.py:89
  222.0 10.9 %copy-start = (f32[7]{0:T(128)S(1)}, f32[7]{0:T(128)}, u32[]{:S(2)}) copy-start(f32[7]{0:T(128)} %param.10) | copy-start | bytes 88
  222.1 11.6 %copy-start.1 = (f32[65]{0:T(128)S(1)}, f32[65]{0:T(128)}, u32[]{:S(2)}) copy-start(f32[65]{0:T(128)} %param.11) | copy-start | bytes 784
  225.5 14.3 %collective-permute-start = (f32[3,32,2048]{2,1,0:T(8,128)S(1)}, f32[3,32,2048]{2,1,0:T(8,128)S(1)}, u32[]{:S(2)}, u32[]{:S(2)}) collective-permute-start(f32[3,32,2048]{2,1,0:T(8,128)S(1)} %bitcast.61), channel_id=1, source_target_pairs={{0,1},{1,2},{2,3},{4,5},{5,6},{6,7},{8,9},{9,10},{10,11},{12,13},{... | collective-permute-start | bytes 2359304 | tf_op jit(solution)/shard_map/ppermute | solution.py:18
  230.9 13.3 %collective-permute-start.1 = (f32[3,32,2048]{2,1,0:T(8,128)S(1)}, f32[3,32,2048]{2,1,0:T(8,128)S(1)}, u32[]{:S(2)}, u32[]{:S(2)}) collective-permute-start(f32[3,32,2048]{2,1,0:T(8,128)S(1)} %bitcast.60), channel_id=1, source_target_pairs={{1,0},{2,1},{3,2},{5,4},{6,5},{7,6},{9,8},{10,9},{11,10},{13,12},{... | collective-permute-start | bytes 2359304 | tf_op jit(solution)/shard_map/ppermute | solution.py:20
where the time goes:
time: 480 us; the launch traced here: 475 us
  waiting for transfers between devices  183 us (38%)
  blocking collectives  112 us (23%)
  local copies, waits for them, and re-layouts  88.5 us (18%)
  other arithmetic  57.4 us (12%)
  starting transfers between devices  19.3 us (4%)
  matrix products  13.8 us (3%)
    all_to_all x1, waiting for transfers between devices, body(): lax.all_to_all(outgoing, 'shot', split_axis=0, concat_axis=0, tiled=True)  174 us
    all_to_all x1, blocking collectives, body(): lax.all_to_all(filtered, 'shot', split_axis=2, concat_axis=1, tiled=True)  112 us
    unnamed x7, local copies, waits for them, and re-layouts  38.7 us
    scatter-add x1, other arithmetic, stack_cells(): jax.ops.segment_sum(received, labels, num_segments=segments + 1)[:segments]  17.4 us
    all_to_all x2, local copies, waits for them, and re-layouts, body(): lax.all_to_all(filtered, 'shot', split_axis=2, concat_axis=1, tiled=True)  16.9 us
    all_to_all x1, other arithmetic, body(): lax.all_to_all(filtered, 'shot', split_axis=2, concat_axis=1, tiled=True)  16.8 us
    dot_general x1, matrix products, block_filter(): jnp.einsum('...ki,io->...ko', extended, table, precision=lax.Precision.HI...  13.8 us
    reshape x1, local copies, waits for them, and re-layouts, block_filter(): return result.reshape(leading + (samples,))  13.1 us
  transfers between devices with their start and end apart: 4, of which 3 were waited for; matrix products, arithmetic and copies ran while one was open for 3% of the time, Pallas kernels for 0%

commit v1 on v0

--- a/solution.py
+++ b/solution.py
@@ -92,7 +92,10 @@
     scaled = stack_cells(received, arrived, sentinel).reshape(off_dev, BOWN, samples)
     mixed = offset_mix(scaled, filter_off)
     filtered = block_filter(mixed, filter_time)
-    relayed = lax.all_to_all(filtered, "shot", split_axis=2, concat_axis=1, tiled=True)
+    relayed = jnp.concatenate(
+        lax.all_to_all(jnp.stack(jnp.split(filtered, lax.axis_size("shot"), axis=2)), "shot", 0, 0),
+        axis=1,
+    )
     return jnp.transpose(relayed, (0, 2, 1))
 
 

time: 480 us -> 407 us (0.85); the launches traced: 475 us -> 406 us
  local copies, waits for them, and re-layouts: 88.5 us -> 39.5 us
  other arithmetic: 57.4 us -> 40.3 us
    unnamed x7 -> x12, local copies, waits for them, and re-layouts: 38.7 us -> 9.14 us
    all_to_all x1 -> x0, other arithmetic: 16.8 us -> none  [body(): lax.all_to_all(filtered, 'shot', split_axis=2, concat_axis=1, tiled=True)]
    all_to_all x2 -> x1, local copies, waits for them, and re-layouts: 16.9 us -> 2.75 us  [body(): lax.all_to_all(jnp.stack(jnp.split(filtered, lax.axis_size('shot'), axis=...]
    reshape x1, local copies, waits for them, and re-layouts: 13.1 us -> 6.72 us  [block_filter(): return result.reshape(leading + (samples,))]
  transfers between devices with their start and end apart: 4 -> 4, of which waited for: 3 -> 3; matrix products, arithmetic and copies ran while one was open for 3% -> 4% of each run, Pallas kernels for 0% -> 0%
where the time goes in v1:
time: 407 us; the launch traced here: 406 us
  waiting for transfers between devices  181 us (44%)
  blocking collectives  112 us (28%)
  other arithmetic  40.3 us (10%)
  local copies, waits for them, and re-layouts  39.5 us (10%)
  starting transfers between devices  19.4 us (5%)
  matrix products  13.8 us (3%)
    all_to_all x1, waiting for transfers between devices, body(): lax.all_to_all(outgoing, 'shot', split_axis=0, concat_axis=0, tiled=True)  174 us
    all_to_all x1, blocking collectives, body(): lax.all_to_all(jnp.stack(jnp.split(filtered, lax.axis_size('shot'), axis=...  112 us
    scatter-add x1, other arithmetic, stack_cells(): jax.ops.segment_sum(received, labels, num_segments=segments + 1)[:segments]  17.4 us
    dot_general x1, matrix products, block_filter(): jnp.einsum('...ki,io->...ko', extended, table, precision=lax.Precision.HI...  13.8 us
    unnamed x12, local copies, waits for them, and re-layouts  9.14 us
    add x1, other arithmetic, offset_mix(): mixed + filter_off[offset_tap] * padded[offset_tap:offset_tap + count]  8.77 us
  transfers between devices with their start and end apart: 4, of which 3 were waited for; matrix products, arithmetic and copies ran while one was open for 4% of the time, Pallas kernels for 0%

profile of v1, /device:TPU:1, one launch (start us, length us, event | category | flops | bytes accessed | tf_op | source)
XLA Modules:
  0.0 406.4 jit_solution(4111863124386256020)
XLA Ops:
  0.0 0.9 select_reduce_fusion.1
  0.9 0.6 reduce-window.6
  1.5 0.2 slice_reduce_fusion
  1.7 0.7 fusion.42
  2.4 0.1 fusion.36
  2.6 2.0 scatter_custom_fusion
  4.5 6.4 %all-to-all-start = ((s32[8,128,1]{1,2,0:T(1,128)}), s32[8,128,1]{1,2,0:T(1,128)S(1)}, u32[]{:S(2)}, u32[]{:S(2)}) async-start(s32[8,128,1]{1,2,0:T(1,128)} %bitcast.8), calls=%async_computation | async-start | bytes 8192 | tf_op jit(solution)/shard_map/all_to_all | solution.py:90
  10.9 6.6 %scatter_custom_fusion.1 = f32[1024,2048]{1,0:T(8,128)} fusion(s32[256]{0:T(256)S(1)} %bitcast.96, f32[256,2048]{1,0:T(8,128)} %param.6, f32[]{:T(128)} %constant.24.clone.1), kind=kCustom, calls=%fused_computation.44 | custom fusion | bytes 8389120 | tf_op jit(solution)/shard_map/scatter | solution.py:86
  17.5 0.0 all-to-all-done
  17.5 5.4 %all-to-all-start.1 = ((f32[8,128,2048]{2,1,0:T(8,128)}), f32[8,128,2048]{2,1,0:T(8,128)}, u32[]{:S(2)}, u32[]{:S(2)}) async-start(f32[8,128,2048]{2,1,0:T(8,128)} %bitcast.85), calls=%async_computation.1 | async-start | bytes 16777216 | tf_op jit(solution)/shard_map/all_to_all | solution.py:89
  22.9 7.8 %scatter_custom_fusion.3 = f32[641]{0:T(1024)S(1)} fusion(s32[1024]{0:T(1024)S(1)} %bitcast.93, f32[1024]{0:T(1024)S(1)} %broadcast.160, f32[]{:T(128)} %constant.24.clone.1), kind=kCustom, calls=%fused_computation.80 | custom fusion | flops 1024 | bytes 2568 | tf_op jit(solution)/shard_map/scatter-add | solution.py:63
  30.8 173.9 %all-to-all-done.1 = f32[8,128,2048]{2,1,0:T(8,128)} async-done(((f32[8,128,2048]{2,1,0:T(8,128)}), f32[8,128,2048]{2,1,0:T(8,128)}, u32[]{:S(2)}, u32[]{:S(2)}) %all-to-all-start.1) | async-done | bytes 8388640 | tf_op jit(solution)/shard_map/all_to_all | solution.py:89
  204.7 17.4 %scatter_custom_fusion.2 = f32[641,2048]{1,0:T(8,128)} fusion(s32[1024]{0:T(1024)S(1)} %bitcast.94, f32[1024,2048]{1,0:T(8,128)} %bitcast.11, f32[]{:T(128)} %constant.24.clone.1), kind=kCustom, calls=%fused_computation.46 | custom fusion | flops 2097152 | bytes 5251584 | tf_op jit(solution)/shard_map/scatter-add | solution.py:62
  222.0 0.0 copy-start
  222.1 0.0 copy-start.1
  222.1 3.3 slice_divide_fusion
  225.3 0.1 fusion.48
  225.5 4.3 %collective-permute-start.1 = (f32[3,32,2048]{2,1,0:T(8,128)S(1)}, f32[3,32,2048]{2,1,0:T(8,128)S(1)}, u32[]{:S(2)}, u32[]{:S(2)}) collective-permute-start(f32[3,32,2048]{2,1,0:T(8,128)S(1)} %bitcast.90), channel_id=1, source_target_pairs={{1,0},{2,1},{3,2},{5,4},{6,5},{7,6},{9,8},{10,9},{11,10},{13,12},{... | collective-permute-start | bytes 2359304 | tf_op jit(solution)/shard_map/ppermute | solution.py:20
  229.8 3.2 collective-permute-start
  233.0 0.0 copy-done
  233.1 0.7 fusion.49
  233.7 0.0 copy-done.1
  233.7 0.8 select_reduce_fusion
  234.5 6.0 %collective-permute-done.1 = f32[3,32,2048]{2,1,0:T(8,128)S(1)} collective-permute-done((f32[3,32,2048]{2,1,0:T(8,128)S(1)}, f32[3,32,2048]{2,1,0:T(8,128)S(1)}, u32[]{:S(2)}, u32[]{:S(2)}) %collective-permute-start.1) | collective-permute-done | bytes 786464 | tf_op jit(solution)/shard_map/ppermute | solution.py:20
  240.6 1.2 collective-permute-done
  241.7 8.8 %fusion.7 = f32[20,32,2048]{2,1,0:T(8,128)S(1)} fusion(f32[20,32,2048]{2,1,0:T(8,128)S(1)} %bitcast.86, f32[3,32,2048]{2,1,0:T(8,128)S(1)} %collective-permute-done.1, f32[3,32,2048]{2,1,0:T(8,128)S(1)} %collective-permute-done, f32[]{:T(128)} %bitcast.20, f32[]{:T(128)} %bitcast.19, f32[]{:T(128)} %bitcast.17, f32[]{:T(128)} %bitcast.16, f32[]{:T(128)} %bitcast.15, ...), kind=kLoop, calls=%fused_computation.25 | loop fusion | flops 24903680 | bytes 12058652 | tf_op jit(solution)/shard_map/add | solution.py:57
  250.5 1.2 copy.23
  251.7 4.2 %fusion.47 = (f32[20,32,15,32]{3,2,1,0:T(8,128)S(1)}, f32[20,32,15,32]{3,2,1,0:T(8,128)}) fusion(f32[20,32,16,128]{3,2,1,0:T(8,128)S(1)} %bitcast.83), kind=kLoop, calls=%fused_computation.102 | loop fusion | bytes 4915200 | tf_op jit(solution)/shard_map/slice | solution.py:43
  256.0 13.8 %fusion = f32[20,32,16,128]{3,2,1,0:T(8,128)} fusion(f32[20,32,15,32]{3,2,1,0:T(8,128)} %get-tuple-element.6, f32[20,32,15,32]{3,2,1,0:T(8,128)S(1)} %get-tuple-element.5, f32[20,32,16,128]{3,2,1,0:T(8,128)S(1)} %bitcast.84, f32[192,128]{1,0:T(8,128)S(1)} %select_reduce_fusion), kind=kOutput, calls=%fused_computation.5 | convolution fusion | flops 3031695360 | bytes 13041664 | tf_op jit(solution)/shard_map/...ki,io->...ko/dot_general | solution.py:47
  269.8 6.7 %reshape.133 = f32[20,32,2048]{2,1,0:T(8,128)} reshape(f32[20,32,16,128]{3,2,1,0:T(8,128)} %fusion) | data formatting | bytes 10485760 | tf_op jit(solution)/shard_map/reshape | solution.py:48
  276.5 1.1 fusion.34
  277.6 1.1 fusion.33
  278.8 1.1 fusion.32
  279.9 1.1 fusion.31
  281.1 1.1 fusion.30
  282.2 1.1 fusion.29
  283.3 1.1 fusion.28
  284.5 1.1 fusion.27
  285.6 112.2 %all_to_all.26 = f32[8,20,32,256]{3,2,1,0:T(8,128)S(1)} all-to-all(f32[8,20,32,256]{3,2,1,0:T(8,128)S(1)} %fusion.27), channel_id=1, replica_groups=mesh['shot'=8,'off'=4] {'shot'}, dimensions={0} | all-to-all | bytes 10485760 | tf_op jit(solution)/shard_map/all_to_all | solution.py:96
  397.8 2.8 copy.20
  400.6 5.9 %copy.21 = f32[20,256,256]{2,1,0:T(8,128)} copy(f32[20,256,256]{1,2,0:T(8,128)} %bitcast.88) | data formatting | bytes 10485760 | tf_op jit(solution)/shard_map/transpose | solution.py:99
  (9 shorter events, 0.1 us)
Async XLA Ops:
  4.5 13.0 %all-to-all-start = ((s32[8,128,1]{1,2,0:T(1,128)}), s32[8,128,1]{1,2,0:T(1,128)S(1)}, u32[]{:S(2)}, u32[]{:S(2)}) async-start(s32[8,128,1]{1,2,0:T(1,128)} %bitcast.8), calls=%async_computation | async-start | bytes 8192 | tf_op jit(solution)/shard_map/all_to_all | solution.py:90
  17.5 187.2 %all-to-all-start.1 = ((f32[8,128,2048]{2,1,0:T(8,128)}), f32[8,128,2048]{2,1,0:T(8,128)}, u32[]{:S(2)}, u32[]{:S(2)}) async-start(f32[8,128,2048]{2,1,0:T(8,128)} %bitcast.85), calls=%async_computation.1 | async-start | bytes 16777216 | tf_op jit(solution)/shard_map/all_to_all | solution.py:89
  222.0 11.0 %copy-start = (f32[7]{0:T(128)S(1)}, f32[7]{0:T(128)}, u32[]{:S(2)}) copy-start(f32[7]{0:T(128)} %param.10) | copy-start | bytes 88
  222.1 11.7 %copy-start.1 = (f32[65]{0:T(128)S(1)}, f32[65]{0:T(128)}, u32[]{:S(2)}) copy-start(f32[65]{0:T(128)} %param.11) | copy-start | bytes 784
  225.5 15.1 %collective-permute-start.1 = (f32[3,32,2048]{2,1,0:T(8,128)S(1)}, f32[3,32,2048]{2,1,0:T(8,128)S(1)}, u32[]{:S(2)}, u32[]{:S(2)}) collective-permute-start(f32[3,32,2048]{2,1,0:T(8,128)S(1)} %bitcast.90), channel_id=1, source_target_pairs={{1,0},{2,1},{3,2},{5,4},{6,5},{7,6},{9,8},{10,9},{11,10},{13,12},{... | collective-permute-start | bytes 2359304 | tf_op jit(solution)/shard_map/ppermute | solution.py:20
  229.8 11.9 %collective-permute-start = (f32[3,32,2048]{2,1,0:T(8,128)S(1)}, f32[3,32,2048]{2,1,0:T(8,128)S(1)}, u32[]{:S(2)}, u32[]{:S(2)}) collective-permute-start(f32[3,32,2048]{2,1,0:T(8,128)S(1)} %bitcast.89), channel_id=1, source_target_pairs={{0,1},{1,2},{2,3},{4,5},{5,6},{6,7},{8,9},{9,10},{10,11},{12,13},{... | collective-permute-start | bytes 2359304 | tf_op jit(solution)/shard_map/ppermute | solution.py:18
